TPU v7x, 256 devices: a whole 4x4x8 slice. The times are simulated.
256 devices in a mesh: users: 64 (over y_lo, x, z), panel: 4 (over y_hi, core).
Axes of the slice: x: 4, y: 4 (y_hi: 2, y_lo: 2; y = y_hi * 2 + y_lo), z: 8, core: 2. Of those that a mesh axis runs over, the one named last changes fastest.
Arguments:
- user_emb0: float32 [65536, 128], P('users'), may hold values from -6 to 6
- item_base: float32 [4, 8192, 128], P('panel'), may hold values from -6 to 6
- weight_tiles: bfloat16 [64, 128, 128], replicated, may hold values from -0.02734375 to 0.02734375
- blk_user: int32 [64, 4, 384], P('users', 'panel'), may hold values from 0 to 7
- blk_item: int32 [64, 4, 384], P('users', 'panel'), may hold values from 0 to 63
- blk_weight: int32 [64, 4, 384], P('users', 'panel'), may hold values from 0 to 63
Outputs:
- user_out: float32 [65536, 128], P('users')
- item_emb: float32 [4, 8192, 128], P('panel', 'users')
All inputs are finite; a program needn't handle non-finite values.
Results may differ from a plain program's by a relative error of at most 0.0036.
Values may be sent and summed in bfloat16 or wider, within the bound.
No kernel may reach another device: no remote copies, remote signals or barrier semaphores. Data moves between devices by JAX's collectives and lax.ppermute only.
A program may use at most 128 MiB of HBM per device.

v0:
```python
import jax
import jax.numpy as jnp
from jax import lax
from jax.sharding import PartitionSpec as P

teleport = 0.2


def item_terms(user_tiles, users, items, weights, weight_tiles, n_items):
    group_size = min(users.shape[0], 128)
    pieces = (
        users.reshape(-1, group_size),
        items.reshape(-1, group_size),
        weights.reshape(-1, group_size),
    )

    def item_add_group(totals, lists):
        tiles = weight_tiles[lists[2]]
        rows = user_tiles[lists[0]]
        products = jnp.einsum("gab,gae->gbe", tiles, rows, preferred_element_type=jnp.float32)
        return (totals + jax.ops.segment_sum(products, lists[1], num_segments=n_items), None)

    start = jnp.zeros((n_items, user_tiles.shape[1], user_tiles.shape[2]), jnp.float32)
    totals, unused = lax.scan(item_add_group, start, pieces)
    return totals


def user_terms(item_tiles, users, items, weights, weight_tiles, n_tiles):
    group_size = min(users.shape[0], 128)
    pieces = (
        users.reshape(-1, group_size),
        items.reshape(-1, group_size),
        weights.reshape(-1, group_size),
    )

    def user_add_group(totals, lists):
        tiles = weight_tiles[lists[2]]
        rows = item_tiles[lists[1]]
        products = jnp.einsum("gab,gbe->gae", tiles, rows, preferred_element_type=jnp.float32)
        return (totals + jax.ops.segment_sum(products, lists[0], num_segments=n_tiles), None)

    start = jnp.zeros((n_tiles, item_tiles.shape[1], item_tiles.shape[2]), jnp.float32)
    totals, unused = lax.scan(user_add_group, start, pieces)
    return totals


def per_device(user_emb0, item_base, weight_tiles, blk_user, blk_item, blk_weight):
    tile_rows = weight_tiles.shape[1]
    width = user_emb0.shape[1]
    n_users = lax.axis_size("users")
    user_tiles = user_emb0.astype(jnp.bfloat16).reshape(-1, tile_rows, width)
    n_user_tiles = user_tiles.shape[0]
    user_list = blk_user.reshape(-1)
    item_list = blk_item.reshape(-1)
    weight_list = blk_weight.reshape(-1)
    partial_value = item_terms(user_tiles, user_list, item_list, weight_list, weight_tiles, n_users)
    partial_flat = partial_value.reshape(n_users * tile_rows, width)
    panel_base = item_base[0]
    position = lax.axis_index("users")
    totals = lax.psum(partial_flat, "users")
    panel_emb = (1.0 - teleport) * totals + teleport * panel_base
    own_emb = lax.dynamic_slice_in_dim(panel_emb, position * tile_rows, tile_rows, 0)
    panel_bf = panel_emb.astype(jnp.bfloat16)
    item_tiles = panel_bf.reshape(n_users, tile_rows, width)
    user_part = user_terms(
        item_tiles, user_list, item_list, weight_list, weight_tiles, n_user_tiles
    )
    user_sum = lax.psum(user_part, "panel")
    user_out = (1.0 - teleport) * user_sum.reshape(-1, width) + teleport * user_emb0
    return (user_out, own_emb[None])


def solution(mesh):
    placed = (
        P("users", None),
        P("panel", None, None),
        P(),
        P("users", "panel", None),
        P("users", "panel", None),
        P("users", "panel", None),
    )
    return jax.shard_map(
        per_device,
        mesh=mesh,
        in_specs=placed,
        out_specs=(P("users", None), P("panel", "users", None)),
        check_vma=False,
    )
```

profile of v0, /device:TPU:1, one launch (start us, length us, event | category | flops | bytes accessed | tf_op | source)
XLA Modules:
  0.0 918.1 jit_solution(14164029038932604751)
XLA Ops:
  7.2 0.0 copy-start.1
  7.2 0.0 all-reduce.3.cloned.1.call-start
  7.2 0.8 reduce
  8.1 0.7 reduce.1
  8.8 0.7 reduce.2
  9.5 1.1 convert_element_type.6
  10.5 2.4 broadcast.84
  13.0 0.0 copy-done.1
  13.0 121.0 %while.20 = (s32[]{:T(128)}, f32[64,128,128]{2,1,0:T(8,128)}, s32[3,128]{1,0:T(4,128)S(1)}, s32[3,128]{1,0:T(4,128)S(1)}, bf16[64,128,128]{2,1,0:T(8,128)(2,1)S(...) while((s32[]{:T(128)}, f32[64,128,128]{2,1,0:T(8,128)}, ...), condition=%wide.region_2.3_spmd, body=%wide.region_0.2_spmd.sunk | while | flops 538970880 | bytes 58734172 | solution.py:24
  13.0 3.1 gather_fusion
  16.1 3.0 gather_fusion.1
  19.1 8.2 fusion.31
  27.3 25.9 %scatter_fusion = f32[64,128,128]{2,1,0:T(8,128)} fusion(f32[64,128,128]{2,1,0:T(8,128)} %get-tuple-element.215, s32[128]{0:T(128)S(1)} %fusion.29, f32[128,128,128]{2,1,0:T(8,128)} %fusion.31), kind=kCustom, calls=%fused_computation.4.clone.1 | custom fusion | flops 2097152 | bytes 25166336 | tf_op jit(solution)/shard_map/while/body/eval_jaxpr/scatter-add | solution.py:21
  53.2 3.1 gather_fusion
  56.3 3.0 gather_fusion.1
  59.3 8.2 fusion.31
  67.5 26.0 %scatter_fusion = f32[64,128,128]{2,1,0:T(8,128)} fusion(f32[64,128,128]{2,1,0:T(8,128)} %get-tuple-element.215, s32[128]{0:T(128)S(1)} %fusion.29, f32[128,128,128]{2,1,0:T(8,128)} %fusion.31), kind=kCustom, calls=%fused_computation.4.clone.1 | custom fusion | flops 2097152 | bytes 25166336 | tf_op jit(solution)/shard_map/while/body/eval_jaxpr/scatter-add | solution.py:21
  93.5 3.1 gather_fusion
  96.6 3.0 gather_fusion.1
  99.6 8.2 fusion.31
  107.9 26.1 %scatter_fusion = f32[64,128,128]{2,1,0:T(8,128)} fusion(f32[64,128,128]{2,1,0:T(8,128)} %get-tuple-element.215, s32[128]{0:T(128)S(1)} %fusion.29, f32[128,128,128]{2,1,0:T(8,128)} %fusion.31), kind=kCustom, calls=%fused_computation.4.clone.1 | custom fusion | flops 2097152 | bytes 25166336 | tf_op jit(solution)/shard_map/while/body/eval_jaxpr/scatter-add | solution.py:21
  134.0 0.0 all-reduce.3.cloned.1.call-update
  134.0 0.0 all-reduce.5.cloned.1.call-start
  134.1 576.4 %all-reduce.3.cloned.1.call-done = f32[8192,128]{1,0:T(8,128)} async-done(((f32[8192,128]{1,0:T(8,128)}), f32[8192,128]{1,0:T(8,128)}) %all-reduce.3.cloned.1.call-update) | async-done | bytes 4194320 | tf_op jit(solution)/shard_map/psum | solution.py:60
  710.5 7.0 fusion.10
  717.5 0.0 copy-start.2
  717.5 98.0 %while.21 = (s32[]{:T(128)}, f32[8,128,128]{2,1,0:T(8,128)S(1)}, s32[3,128]{1,0:T(4,128)S(1)}, s32[3,128]{1,0:T(4,128)S(1)}, bf16[64,128,128]{2,1,0:T(8,128)(2,1...) while((s32[]{:T(128)}, f32[8,128,128]{2,1,0:T(8,128)S(1)}, ...), condition=%wide.region_6.7_spmd, body=%wide.region_4.6_spmd.sunk | while | flops 538970880 | bytes 58734172 | solution.py:43
  717.5 3.0 gather_fusion.2
  720.6 4.6 gather_fusion.3
  725.2 7.9 fusion.36
  733.1 17.0 %scatter_fusion.1 = f32[8,128,128]{2,1,0:T(8,128)S(1)} fusion(f32[8,128,128]{2,1,0:T(8,128)S(1)} %get-tuple-element.239, s32[128]{0:T(128)S(1)} %fusion.34, f32[128,128,128]{2,1,0:T(8,128)} %fusion.36), kind=kCustom, calls=%fused_computation.5.clone.1 | custom fusion | flops 2097152 | bytes 25166336 | tf_op jit(solution)/shard_map/while/body/eval_jaxpr/scatter-add | solution.py:40
  750.2 3.0 gather_fusion.2
  753.3 4.6 gather_fusion.3
  757.9 7.9 fusion.36
  765.8 17.0 %scatter_fusion.1 = f32[8,128,128]{2,1,0:T(8,128)S(1)} fusion(f32[8,128,128]{2,1,0:T(8,128)S(1)} %get-tuple-element.239, s32[128]{0:T(128)S(1)} %fusion.34, f32[128,128,128]{2,1,0:T(8,128)} %fusion.36), kind=kCustom, calls=%fused_computation.5.clone.1 | custom fusion | flops 2097152 | bytes 25166336 | tf_op jit(solution)/shard_map/while/body/eval_jaxpr/scatter-add | solution.py:40
  782.9 3.0 gather_fusion.2
  785.9 4.6 gather_fusion.3
  790.5 7.9 fusion.36
  798.5 17.0 %scatter_fusion.1 = f32[8,128,128]{2,1,0:T(8,128)S(1)} fusion(f32[8,128,128]{2,1,0:T(8,128)S(1)} %get-tuple-element.239, s32[128]{0:T(128)S(1)} %fusion.34, f32[128,128,128]{2,1,0:T(8,128)} %fusion.36), kind=kCustom, calls=%fused_computation.5.clone.1 | custom fusion | flops 2097152 | bytes 25166336 | tf_op jit(solution)/shard_map/while/body/eval_jaxpr/scatter-add | solution.py:40
  815.5 0.0 copy-start
  815.5 0.8 copy-done
  816.3 0.0 all-reduce.5.cloned.1.call-update
  816.3 1.5 dynamic-slice_bitcast_fusion
  817.8 91.5 %all-reduce.5.cloned.1.call-done = f32[8,128,128]{2,1,0:T(8,128)} async-done(((f32[8,128,128]{2,1,0:T(8,128)}), f32[8,128,128]{2,1,0:T(8,128)}) %all-reduce.5.cloned.1.call-update) | async-done | bytes 524304 | tf_op jit(solution)/shard_map/psum | solution.py:68
  909.3 1.1 broadcast_multiply_fusion
  910.4 0.0 copy-done.2
  910.4 0.9 bitcast_add_fusion.1
  (25 shorter events, 0.2 us)
Async XLA Ops:
  7.2 5.8 copy-start.1
  7.2 703.3 %all-reduce.3.cloned.1.call-start = ((), (), s32[]{:S(2)}) async-start(), calls=%async_computation | async-start | bytes 8388608 | tf_op jit(solution)/shard_map/psum | solution.py:60
  134.0 775.3 %all-reduce.5.cloned.1.call-start = ((), (), s32[]{:S(2)}) async-start(), calls=%async_computation.1 | async-start | bytes 1048576 | tf_op jit(solution)/shard_map/psum | solution.py:68
  717.5 192.9 %copy-start.2 = (f32[1024,128]{1,0:T(8,128)S(1)}, f32[1024,128]{1,0:T(8,128)}, u32[]{:S(2)}) copy-start(f32[1024,128]{1,0:T(8,128)} %param.10) | copy-start | bytes 1572868
  815.5 0.8 copy-start
Sparse Core Ops, SparseCore 0:
  134.1 576.2 all-reduce.2
  816.4 92.7 all-reduce.4
where the time goes:
time: 920 us; the launch traced here: 918 us
  waiting for transfers between devices  668 us (73%)
  other arithmetic  141 us (15%)
  matrix products  48.5 us (5%)
  local copies, waits for them, and re-layouts  46 us (5%)
  between operations  14.1 us (2%)
    psum x1, waiting for transfers between devices, per_device(): totals = lax.psum(partial_flat, 'users')  576 us
    psum x1, waiting for transfers between devices, per_device(): user_sum = lax.psum(user_part, 'panel')  91.5 us
    scatter-add x3, other arithmetic, item_add_group(): jax.ops.segment_sum(products, lists[1], num_segments=n_items)  78 us
    scatter-add x3, other arithmetic, user_add_group(): jax.ops.segment_sum(products, lists[0], num_segments=n_tiles)  51.1 us
    dot_general x3, matrix products, item_add_group(): jnp.einsum('gab,gae->gbe', tiles, rows, preferred_element_type=jnp.float32)  24.7 us
    dot_general x3, matrix products, user_add_group(): jnp.einsum('gab,gbe->gae', tiles, rows, preferred_element_type=jnp.float32)  23.8 us
  transfers between devices with their start and end apart: 2, of which 2 were waited for; matrix products, arithmetic and copies ran while one was open for 0% of the time, Pallas kernels for 0%

commit v1 on v0

--- a/solution.py
+++ b/solution.py
@@ -1,9 +1,18 @@
+import functools
 import jax
 import jax.numpy as jnp
 from jax import lax
 from jax.sharding import PartitionSpec as P
 
 teleport = 0.2
+
+
+def save_joints(frame_in, axis_id):
+    item_now = lax.all_gather(frame_in, axis_id)
+    return jnp.sum(item_now, 0)
+
+
+_search_row = functools.partial(save_joints, axis_id="panel")
 
 
 def item_terms(user_tiles, users, items, weights, weight_tiles, n_items):
@@ -65,7 +74,7 @@
     user_part = user_terms(
         item_tiles, user_list, item_list, weight_list, weight_tiles, n_user_tiles
     )
-    user_sum = lax.psum(user_part, "panel")
+    user_sum = _search_row(user_part)
     user_out = (1.0 - teleport) * user_sum.reshape(-1, width) + teleport * user_emb0
     return (user_out, own_emb[None])
 

time: 920 us -> 902 us (0.980)
  waiting for transfers between devices: 668 us -> 649 us
    psum x1 -> x0, waiting for transfers between devices: 91.5 us -> none  [per_device(): user_sum = lax.psum(user_part, 'panel')]
    all_gather x0 -> x1, waiting for transfers between devices: none -> 73 us  [save_joints(): item_now = lax.all_gather(frame_in, axis_id)]
where the time goes in v1:
time: 902 us; the launch traced here: 900 us
  waiting for transfers between devices  649 us (72%)
  other arithmetic  142 us (16%)
  matrix products  48.5 us (5%)
  local copies, waits for them, and re-layouts  46 us (5%)
  between operations  14.1 us (2%)
    psum x1, waiting for transfers between devices, per_device(): totals = lax.psum(partial_flat, 'users')  576 us
    scatter-add x3, other arithmetic, item_add_group(): jax.ops.segment_sum(products, lists[1], num_segments=n_items)  78 us
    all_gather x1, waiting for transfers between devices, save_joints(): item_now = lax.all_gather(frame_in, axis_id)  73 us
    scatter-add x3, other arithmetic, user_add_group(): jax.ops.segment_sum(products, lists[0], num_segments=n_tiles)  51.1 us
    dot_general x3, matrix products, item_add_group(): jnp.einsum('gab,gae->gbe', tiles, rows, preferred_element_type=jnp.float32)  24.7 us
    dot_general x3, matrix products, user_add_group(): jnp.einsum('gab,gbe->gae', tiles, rows, preferred_element_type=jnp.float32)  23.8 us
  transfers between devices with their start and end apart: 2, of which 2 were waited for; matrix products, arithmetic and copies ran while one was open for 0% of the time, Pallas kernels for 0%

profile of v1, /device:TPU:1, one launch (start us, length us, event | category | flops | bytes accessed | tf_op | source)
XLA Modules:
  0.0 900.3 jit_solution(7347126226761411298)
XLA Ops:
  7.2 0.0 copy-start.1
  7.2 0.0 all-reduce.2.cloned.1.call-start
  7.2 0.8 reduce
  8.1 0.7 reduce.1
  8.8 0.7 reduce.2
  9.5 1.1 convert_element_type.6
  10.5 2.4 broadcast.84
  13.0 0.0 copy-done.1
  13.0 121.0 %while.20 = (s32[]{:T(128)}, f32[64,128,128]{2,1,0:T(8,128)}, s32[3,128]{1,0:T(4,128)S(1)}, s32[3,128]{1,0:T(4,128)S(1)}, bf16[64,128,128]{2,1,0:T(8,128)(2,1)S(...) while((s32[]{:T(128)}, f32[64,128,128]{2,1,0:T(8,128)}, ...), condition=%wide.region_2.3_spmd, body=%wide.region_0.2_spmd.sunk | while | flops 538970880 | bytes 58734172 | solution.py:33
  13.0 3.1 gather_fusion
  16.1 3.0 gather_fusion.1
  19.1 8.2 fusion.31
  27.3 25.9 %scatter_fusion = f32[64,128,128]{2,1,0:T(8,128)} fusion(f32[64,128,128]{2,1,0:T(8,128)} %get-tuple-element.215, s32[128]{0:T(128)S(1)} %fusion.29, f32[128,128,128]{2,1,0:T(8,128)} %fusion.31), kind=kCustom, calls=%fused_computation.4.clone.1 | custom fusion | flops 2097152 | bytes 25166336 | tf_op jit(solution)/shard_map/while/body/eval_jaxpr/scatter-add | solution.py:30
  53.2 3.1 gather_fusion
  56.3 3.0 gather_fusion.1
  59.3 8.2 fusion.31
  67.5 26.0 %scatter_fusion = f32[64,128,128]{2,1,0:T(8,128)} fusion(f32[64,128,128]{2,1,0:T(8,128)} %get-tuple-element.215, s32[128]{0:T(128)S(1)} %fusion.29, f32[128,128,128]{2,1,0:T(8,128)} %fusion.31), kind=kCustom, calls=%fused_computation.4.clone.1 | custom fusion | flops 2097152 | bytes 25166336 | tf_op jit(solution)/shard_map/while/body/eval_jaxpr/scatter-add | solution.py:30
  93.5 3.1 gather_fusion
  96.6 3.0 gather_fusion.1
  99.6 8.2 fusion.31
  107.9 26.1 %scatter_fusion = f32[64,128,128]{2,1,0:T(8,128)} fusion(f32[64,128,128]{2,1,0:T(8,128)} %get-tuple-element.215, s32[128]{0:T(128)S(1)} %fusion.29, f32[128,128,128]{2,1,0:T(8,128)} %fusion.31), kind=kCustom, calls=%fused_computation.4.clone.1 | custom fusion | flops 2097152 | bytes 25166336 | tf_op jit(solution)/shard_map/while/body/eval_jaxpr/scatter-add | solution.py:30
  134.0 0.0 all-reduce.2.cloned.1.call-update
  134.0 0.0 all-gather.3.cloned.1.call-start
  134.1 576.4 %all-reduce.2.cloned.1.call-done = f32[8192,128]{1,0:T(8,128)} async-done(((f32[8192,128]{1,0:T(8,128)}), f32[8192,128]{1,0:T(8,128)}) %all-reduce.2.cloned.1.call-update) | async-done | bytes 4194320 | tf_op jit(solution)/shard_map/psum | solution.py:69
  710.5 7.0 fusion.10
  717.5 98.0 %while.21 = (s32[]{:T(128)}, f32[8,128,128]{2,1,0:T(8,128)S(1)}, s32[3,128]{1,0:T(4,128)S(1)}, s32[3,128]{1,0:T(4,128)S(1)}, bf16[64,128,128]{2,1,0:T(8,128)(2,1...) while((s32[]{:T(128)}, f32[8,128,128]{2,1,0:T(8,128)S(1)}, ...), condition=%wide.region_6.7_spmd, body=%wide.region_4.6_spmd.sunk | while | flops 538970880 | bytes 58734172 | solution.py:52
  717.5 3.0 gather_fusion.2
  720.6 4.6 gather_fusion.3
  725.2 7.9 fusion.36
  733.1 17.0 %scatter_fusion.1 = f32[8,128,128]{2,1,0:T(8,128)S(1)} fusion(f32[8,128,128]{2,1,0:T(8,128)S(1)} %get-tuple-element.239, s32[128]{0:T(128)S(1)} %fusion.34, f32[128,128,128]{2,1,0:T(8,128)} %fusion.36), kind=kCustom, calls=%fused_computation.5.clone.1 | custom fusion | flops 2097152 | bytes 25166336 | tf_op jit(solution)/shard_map/while/body/eval_jaxpr/scatter-add | solution.py:49
  750.2 3.0 gather_fusion.2
  753.3 4.6 gather_fusion.3
  757.8 7.9 fusion.36
  765.8 17.0 %scatter_fusion.1 = f32[8,128,128]{2,1,0:T(8,128)S(1)} fusion(f32[8,128,128]{2,1,0:T(8,128)S(1)} %get-tuple-element.239, s32[128]{0:T(128)S(1)} %fusion.34, f32[128,128,128]{2,1,0:T(8,128)} %fusion.36), kind=kCustom, calls=%fused_computation.5.clone.1 | custom fusion | flops 2097152 | bytes 25166336 | tf_op jit(solution)/shard_map/while/body/eval_jaxpr/scatter-add | solution.py:49
  782.9 3.0 gather_fusion.2
  785.9 4.6 gather_fusion.3
  790.5 7.9 fusion.36
  798.5 17.0 %scatter_fusion.1 = f32[8,128,128]{2,1,0:T(8,128)S(1)} fusion(f32[8,128,128]{2,1,0:T(8,128)S(1)} %get-tuple-element.239, s32[128]{0:T(128)S(1)} %fusion.34, f32[128,128,128]{2,1,0:T(8,128)} %fusion.36), kind=kCustom, calls=%fused_computation.5.clone.1 | custom fusion | flops 2097152 | bytes 25166336 | tf_op jit(solution)/shard_map/while/body/eval_jaxpr/scatter-add | solution.py:49
  815.5 0.0 copy-start
  815.5 0.0 copy-start.2
  815.5 0.8 copy-done
  816.3 0.0 all-gather.3.cloned.1.call-update
  816.3 1.5 dynamic-slice_bitcast_fusion
  817.8 73.0 %all-gather.3.cloned.1.call-done = f32[32,128,128]{2,1,0:T(8,128)} async-done(((f32[8,128,128]{2,1,0:T(8,128)}), f32[32,128,128]{2,1,0:T(8,128)}) %all-gather.3.cloned.1.call-update) | async-done | bytes 2097168 | tf_op jit(solution)/shard_map/all_gather | solution.py:11
  890.8 1.8 reduce_sum.9
  892.6 0.0 copy-done.2
  892.6 0.9 bitcast_add_fusion.1
  (26 shorter events, 0.2 us)
Async XLA Ops:
  7.2 5.8 copy-start.1
  7.2 703.3 %all-reduce.2.cloned.1.call-start = ((), (), s32[]{:S(2)}) async-start(), calls=%async_computation | async-start | bytes 8388608 | tf_op jit(solution)/shard_map/psum | solution.py:69
  134.0 756.7 %all-gather.3.cloned.1.call-start = ((), (), s32[]{:S(2)}) async-start(), calls=%async_computation.1 | async-start | bytes 2621440 | tf_op jit(solution)/shard_map/all_gather | solution.py:11
  815.5 0.8 copy-start
  815.5 77.1 %copy-start.2 = (f32[1024,128]{1,0:T(8,128)S(1)}, f32[1024,128]{1,0:T(8,128)}, u32[]{:S(2)}) copy-start(f32[1024,128]{1,0:T(8,128)} %param.10) | copy-start | bytes 1572868
Sparse Core Ops, SparseCore 0:
  134.1 576.2 all-reduce.1
  816.4 74.2 all-gather.2
